TPU v7x, 512 devices: a whole 4x4x16 slice. The times are simulated.
512 devices in a mesh: pole: 2 (over core), prow: 16 (over z), pcol: 16 (over x, y).
Axes of the slice: x: 4, y: 4, z: 16, core: 2. Of those that a mesh axis runs over, the one named last changes fastest.
Arguments:
- inverse_trailing: float32 [32768, 16384], P(('pole', 'prow'), 'pcol'), parts along dimension 0, may hold values from -6 to 6
- factor_blocks: float32 [6, 4096, 256], P('pole', 'prow'), parts along dimension 0, may hold values from -0.09375 to 0.09375
- diag_pivots: float32 [256, 6, 256], P('pcol', 'pole'), parts along dimension 1, may hold values from -6 to 6
- structure: int32 [3, 16], replicated, may hold values from 0 to 63, as said below
- owner_map: int32 [64], replicated, may hold values from 0 to 63, each once
Outputs:
- row_inverse: float32 [256, 6, 16384], P('pcol', 'pole', 'prow'), parts along dimension 1
- diag_inverse: float32 [256, 6, 256], P('pcol', 'pole'), parts along dimension 1
There are 2 independent parts, one for each index of `pole`. A program takes and returns all parts, laid end to end along the dimension named above; an argument that names none is the same for every part. Nothing has to cross between parts.
Inputs may be any that keep to these rules, and one draw needn't show every extreme that they name: `structure`: each row lists 16 distinct logical ancestor blocks.
All inputs are finite; a program needn't handle non-finite values.
Results may differ from a plain program's by a relative error of at most 0.0001.
Values sent between devices are 32-bit elements; how exact they have to be, the bound alone decides.
No kernel may reach another device: no remote copies, remote signals or barrier semaphores. Data moves between devices by JAX's collectives and lax.ppermute only.
A program may use at most 64 MiB of HBM per device.

v0:
```python
import jax
import jax.numpy as jnp
from jax import lax
from jax.sharding import PartitionSpec as P


def diag_product(values, factor):
    return jnp.einsum("awj,wjb->awb", values, factor, precision=lax.Precision.HIGHEST)


def shards(inverse_trailing, factor_blocks, diag_pivots, structure, owner_map):
    width = factor_blocks.shape[2]
    window = factor_blocks.shape[0]
    owned = inverse_trailing.shape[0] // width
    ancestors = owner_map.shape[0]
    row_index = lax.axis_index("prow")
    col_index = lax.axis_index("pcol")
    catalog = jnp.arange(ancestors, dtype=jnp.int32)
    positions = jnp.sum(
        jnp.where(structure[:, :, None] == catalog[None, None, :], owner_map[None, None, :], 0),
        axis=2,
    )
    slots = jnp.arange(owned, dtype=jnp.int32)
    col_slots = col_index * owned + slots
    row_slots = row_index * owned + slots
    piece = lax.all_gather(factor_blocks, "prow", axis=1, tiled=True)
    count = piece.shape[1] // width
    blocks = piece.reshape(window, count, width, width)
    col_pick = (positions[:, None, :] == col_slots[None, :, None]).astype(jnp.float32)
    row_pick = (positions[:, None, :] == row_slots[None, :, None]).astype(jnp.float32)
    col_acc = jnp.einsum("wsi,wiab->wsab", col_pick, blocks, precision=lax.Precision.HIGHEST)
    row_acc = jnp.einsum("wsi,wiab->wsab", row_pick, blocks, precision=lax.Precision.HIGHEST)
    col_factor = col_acc.reshape(window, owned * width, width)
    row_factor = row_acc.reshape(window, owned * width, width)
    in_rows = jnp.any(positions[:, None, :] == row_slots[None, :, None], axis=2).astype(jnp.float32)
    row_mask = jnp.repeat(in_rows, width, axis=1)
    summed = lax.psum_scatter(
        -jnp.einsum("wja,ij->awi", col_factor, inverse_trailing, precision=lax.Precision.HIGHEST),
        "pcol",
        scatter_dimension=0,
        tiled=True,
    )
    row_inverse = summed * row_mask[None, :, :]
    local_diag = diag_product(row_inverse, row_factor)
    total_diag = lax.psum(local_diag, "prow")
    diag_inverse = diag_pivots - total_diag
    return (row_inverse, diag_inverse)


def solution(mesh):
    in_specs = (
        P(("pole", "prow"), "pcol"),
        P("pole", "prow", None),
        P("pcol", "pole", None),
        P(),
        P(),
    )
    out_specs = (P("pcol", "pole", "prow"), P("pcol", "pole", None))
    return jax.shard_map(shards, mesh=mesh, in_specs=in_specs, out_specs=out_specs, check_vma=False)
```

profile of v0, /device:TPU:2, one launch (start us, length us, event | category | flops | bytes accessed | tf_op | source)
XLA Modules:
  0.0 359.3 jit_solution(15618497550631797289)
XLA Ops:
  7.2 0.0 all-gather.2.cloned.1.call-start
  7.2 0.7 all-gather.2.cloned.1.call-update
  7.9 0.0 reduce-scatter.2.cloned.1.call-start
  8.0 0.9 select_reduce_fusion
  8.9 153.8 %all-gather.2.cloned.1.call-done = f32[3,4096,256]{2,1,0:T(8,128)} async-done(((f32[3,256,256]{2,1,0:T(8,128)}), f32[3,4096,256]{2,1,0:T(8,128)}) %all-gather.2.cloned.1.call-update) | async-done | bytes 12582928 | tf_op jit(solution)/shard_map/all_gather | solution.py:26
  162.6 16.1 %fusion.2 = f32[3,4,256,256]{3,1,2,0:T(4,128)S(1)} fusion(f32[3,16,256,256]{3,2,1,0:T(8,128)} %bitcast.28, s32[3,16]{1,0:T(4,128)S(1)} %select_reduce_fusion, s32[4]{0:T(128)S(1)} %iota_add_fusion.1), kind=kOutput, calls=%fused_computation.2 | convolution fusion | flops 150995136 | bytes 15728848 | tf_op jit(solution)/shard_map/wsi,wiab->wsab/dot_general | solution.py:31
  178.8 0.0 copy-start
  178.8 0.5 copy.13
  179.3 1.6 copy-done
  181.0 22.3 %negate_bitcast_fusion = f32[256,3,1024]{2,0,1:T(8,128)} fusion(f32[3,1024,256]{2,1,0:T(8,128)S(1)} %bitcast.31, f32[1024,1024]{1,0:T(8,128)S(1)} %copy-done), kind=kOutput, calls=%fused_computation.6 | convolution fusion | flops 9664462848 | bytes 10485760 | tf_op jit(solution)/shard_map/wja,ij->awi/dot_general | solution.py:38
  203.3 0.0 reduce-scatter.2.cloned.1.call-update
  203.3 0.2 compare_reduce_fusion
  203.5 0.1 broadcast_bitcast_fusion
  203.6 15.8 %fusion = f32[3,4,256,256]{3,1,2,0:T(4,128)S(1)} fusion(f32[3,16,256,256]{3,2,1,0:T(8,128)} %bitcast.29, s32[3,16]{1,0:T(4,128)S(1)} %select_reduce_fusion, s32[4]{0:T(128)S(1)} %iota_add_fusion), kind=kOutput, calls=%fused_computation | convolution fusion | flops 150995136 | bytes 15728848 | tf_op jit(solution)/shard_map/wsi,wiab->wsab/dot_general | solution.py:32
  219.4 0.5 copy.16
  220.0 0.0 copy-start.2
  220.0 72.0 %reduce-scatter.2.cloned.1.call-done = f32[16,3,1024]{2,0,1:T(8,128)} async-done(((f32[256,3,1024]{2,0,1:T(8,128)}), f32[16,3,1024]{2,0,1:T(8,128)}) %reduce-scatter.2.cloned.1.call-update) | async-done | bytes 196624 | tf_op jit(solution)/shard_map/reduce_scatter | solution.py:37
  292.0 0.9 broadcast_multiply_fusion
  293.0 0.0 copy-start.1
  293.0 1.7 convolution_bitcast_fusion
  294.7 56.9 %psum.7 = f32[16,3,256]{2,0,1:T(8,128)S(1)} all-reduce(f32[16,3,256]{2,0,1:T(8,128)S(1)} %convolution_bitcast_fusion), channel_id=1, replica_groups=mesh['pole'=2,'prow'=16,'pcol'=16] {'prow'}, use_global_device_ids=true, to_apply=%region_3.4 | all-reduce | flops 12288 | bytes 98304 | tf_op jit(solution)/shard_map/psum | solution.py:45
  351.6 0.0 copy-done.2
  351.6 0.6 sub.3
  352.2 0.0 copy-done.1
  (4 shorter events, 0.0 us)
Async XLA Ops:
  7.2 155.5 %all-gather.2.cloned.1.call-start = ((), (), s32[]{:S(2)}) async-start(), calls=%async_computation.1 | async-start | bytes 13369344 | tf_op jit(solution)/shard_map/all_gather | solution.py:26
  7.9 284.1 %reduce-scatter.2.cloned.1.call-start = ((), (), s32[]{:S(2)}) async-start(), calls=%async_computation.2 | async-start | bytes 3342336 | tf_op jit(solution)/shard_map/reduce_scatter | solution.py:37
  178.8 2.2 copy-start
  220.0 131.6 %copy-start.2 = (f32[16,3,256]{2,0,1:T(8,128)S(1)}, f32[16,3,256]{2,0,1:T(8,128)}, u32[]{:S(2)}) copy-start(f32[16,3,256]{2,0,1:T(8,128)} %param.7) | copy-start | bytes 147460
  293.0 59.3 %copy-start.1 = (f32[16,3,1024]{2,0,1:T(8,128)}, f32[16,3,1024]{2,0,1:T(8,128)S(1)}, u32[]{:S(2)}) copy-start(f32[16,3,1024]{2,0,1:T(8,128)S(1)} %broadcast_multiply_fusion) | copy-start | bytes 589828
Sparse Core Ops, SparseCore 0:
  10.1 152.5 all-gather.1
  203.4 88.5 reduce-scatter.1
where the time goes:
time: 365 us; the launch traced here: 359 us
  waiting for transfers between devices  226 us (62%)
  blocking collectives  56.9 us (16%)
  matrix products  56 us (15%)
  between operations  14.4 us (4%)
    all_gather x1, waiting for transfers between devices, shards(): piece = lax.all_gather(factor_blocks, 'prow', axis=1, tiled=True)  154 us
    reduce_scatter x1, waiting for transfers between devices, shards(): lax.psum_scatter(-jnp.einsum('wja,ij->awi', col_factor, inverse_trailing,...  72 us
    psum x1, blocking collectives, shards(): total_diag = lax.psum(local_diag, 'prow')  56.9 us
    dot_general x1, matrix products, shards(): jnp.einsum('wja,ij->awi', col_factor, inverse_trailing, precision=lax.Pre...  22.3 us
    dot_general x1, matrix products, shards(): jnp.einsum('wsi,wiab->wsab', col_pick, blocks, precision=lax.Precision.HI...  16.1 us
    dot_general x1, matrix products, shards(): jnp.einsum('wsi,wiab->wsab', row_pick, blocks, precision=lax.Precision.HI...  15.8 us
  transfers between devices with their start and end apart: 2, of which 2 were waited for; matrix products, arithmetic and copies ran while one was open for 5% of the time, Pallas kernels for 0%

commit v1 on v0

v1 whole, which is shorter than its diff:
```python
import jax
import jax.numpy as jnp
from jax import lax
from jax.sharding import PartitionSpec as P


def diag_product(values, factor):
    return jnp.einsum("awj,wjb->awb", values, factor, precision=lax.Precision.HIGHEST)


def pick_blocks(blocks, positions, slots):
    window = blocks.shape[0]
    match = positions[:, None, :] == slots[None, :, None]
    index = jnp.argmax(match, axis=2)
    present = jnp.any(match, axis=2)
    chosen = blocks[jnp.arange(window)[:, None], index]
    return jnp.where(present[:, :, None, None], chosen, 0.0), present


def make_shards(prow_size, pcol_size):
    def shards(inverse_trailing, factor_blocks, diag_pivots, structure, owner_map):
        width = factor_blocks.shape[2]
        window = factor_blocks.shape[0]
        local_rows = factor_blocks.shape[1]
        owned = inverse_trailing.shape[0] // width
        row_index = lax.axis_index("prow")
        col_index = lax.axis_index("pcol")
        positions = jnp.take(owner_map, structure, axis=0)
        slots = jnp.arange(owned, dtype=jnp.int32)
        col_slots = col_index * owned + slots
        row_slots = row_index * owned + slots
        segment = local_rows // pcol_size
        mine = lax.dynamic_slice_in_dim(factor_blocks, col_index * segment, segment, axis=1)
        piece = lax.all_gather(mine, ("prow", "pcol"), axis=1, tiled=True)
        count = piece.shape[1] // width
        blocks = piece.reshape(window, count, width, width)
        col_acc, _ = pick_blocks(blocks, positions, col_slots)
        row_acc, in_rows = pick_blocks(blocks, positions, row_slots)
        col_factor = col_acc.reshape(window, owned * width, width)
        row_factor = row_acc.reshape(window, owned * width, width)
        row_mask = jnp.repeat(in_rows.astype(jnp.float32), width, axis=1)
        summed = lax.psum_scatter(
            -jnp.einsum("wja,ij->awi", col_factor, inverse_trailing, precision=lax.Precision.HIGHEST),
            "pcol",
            scatter_dimension=0,
            tiled=True,
        )
        row_inverse = summed * row_mask[None, :, :]
        local_diag = diag_product(row_inverse, row_factor)
        gathered = lax.all_gather(local_diag, "prow", axis=0, tiled=False)
        total_diag = jnp.sum(gathered, axis=0)
        diag_inverse = diag_pivots - total_diag
        return (row_inverse, diag_inverse)

    return shards


def solution(mesh):
    in_specs = (
        P(("pole", "prow"), "pcol"),
        P("pole", "prow", None),
        P("pcol", "pole", None),
        P(),
        P(),
    )
    out_specs = (P("pcol", "pole", "prow"), P("pcol", "pole", None))
    shards = make_shards(mesh.shape["prow"], mesh.shape["pcol"])
    return jax.shard_map(shards, mesh=mesh, in_specs=in_specs, out_specs=out_specs, check_vma=False)
```

time: 365 us -> 410 us (1.12); the launches traced: 359 us -> 410 us
  waiting for transfers between devices: 226 us -> 306 us
  matrix products: 56 us -> 26 us
  blocking collectives: 56.9 us -> 34.9 us
  local copies, waits for them, and re-layouts: 2.81 us -> 18.6 us
  other arithmetic: 2.71 us -> 10.5 us
    all_gather x1, waiting for transfers between devices: 154 us -> 232 us  [shards(): piece = lax.all_gather(mine, ('prow', 'pcol'), axis=1, tiled=True)]
    psum x1 -> x0, blocking collectives: 56.9 us -> none  [shards(): total_diag = lax.psum(local_diag, 'prow')]
    all_gather x0 -> x1, blocking collectives: none -> 34.9 us  [shards(): gathered = lax.all_gather(local_diag, 'prow', axis=0, tiled=False)]
    dot_general x2 -> x0, matrix products: 32 us -> none  [the longest x1 16.1 us: shards(): jnp.einsum('wsi,wiab->wsab', col_pick, blocks, precision=lax.Precision.HI...]
    gather x0 -> x4, local copies, waits for them, and re-layouts: none -> 15.6 us  [the longest x2 14.1 us: pick_blocks(): chosen = blocks[jnp.arange(window)[:, None], index]]
    select_n x0 -> x4, other arithmetic: none -> 7.09 us  [the longest x2 5.71 us: pick_blocks(): return (jnp.where(present[:, :, None, None], chosen, 0.0), present)]
  transfers between devices with their start and end apart: 2 -> 2, of which waited for: 2 -> 2; matrix products, arithmetic and copies ran while one was open for 5% -> 4% of each run, Pallas kernels for 0% -> 0%
where the time goes in v1:
time: 410 us
  waiting for transfers between devices  306 us (75%)
  blocking collectives  34.9 us (9%)
  matrix products  26 us (6%)
  local copies, waits for them, and re-layouts  18.6 us (5%)
  between operations  14.1 us (3%)
  other arithmetic  10.5 us (3%)
    all_gather x1, waiting for transfers between devices, shards(): piece = lax.all_gather(mine, ('prow', 'pcol'), axis=1, tiled=True)  232 us
    reduce_scatter x1, waiting for transfers between devices, shards(): lax.psum_scatter(-jnp.einsum('wja,ij->awi', col_factor, inverse_trailing,...  74 us
    all_gather x1, blocking collectives, shards(): gathered = lax.all_gather(local_diag, 'prow', axis=0, tiled=False)  34.9 us
    dot_general x1, matrix products, shards(): jnp.einsum('wja,ij->awi', col_factor, inverse_trailing, precision=lax.Pre...  22.3 us
    gather x2, local copies, waits for them, and re-layouts, pick_blocks(): chosen = blocks[jnp.arange(window)[:, None], index]  14.1 us
  transfers between devices with their start and end apart: 2, of which 2 were waited for; matrix products, arithmetic and copies ran while one was open for 4% of the time, Pallas kernels for 0%

profile of v1, /device:TPU:2, one launch (start us, length us, event | category | flops | bytes accessed | tf_op | source)
XLA Modules:
  0.0 410.0 jit_solution(18204326391388806719)
XLA Ops:
  7.2 1.1 copy-done
  8.3 0.6 constant_dynamic-slice_fusion
  9.0 0.7 compare_select_fusion.2
  9.7 0.1 reshape.38
  9.8 1.4 gather_fusion
  11.2 0.1 reshape.37
  11.3 0.7 and_select_fusion
  12.0 0.7 compare_reduce_fusion.2
  12.7 0.1 reshape.44
  12.8 0.3 compare_reduce_fusion.1
  13.2 231.9 %all-gather.3.cloned.1.call-done = f32[3,4096,256]{2,1,0:T(8,128)} async-done(((f32[3,16,256]{2,1,0:T(8,128)}), f32[3,4096,256]{2,1,0:T(8,128)}) %all-gather.3.cloned.1.call-update) | async-done | bytes 12582928 | tf_op jit(solution)/shard_map/all_gather | solution.py:34
  245.1 7.1 %gather_fusion.1 = f32[12,256,256]{2,1,0:T(8,128)} fusion(f32[3,16,256,256]{3,2,1,0:T(8,128)} %bitcast.43, s32[12]{0:T(128)S(1)} %reshape.44), kind=kCustom, calls=%fused_computation.1 | custom fusion | bytes 6291552 | tf_op jit(solution)/shard_map/gather | solution.py:16
  252.1 2.3 bitcast_select_fusion.1
  254.5 0.8 copy-done.1
  255.3 22.3 %negate_bitcast_fusion = f32[256,3,1024]{2,0,1:T(8,128)} fusion(f32[3,1024,256]{2,1,0:T(8,128)S(1)} %bitcast_select_fusion.1, f32[1024,1024]{1,0:T(8,128)S(1)} %copy-done.1), kind=kOutput, calls=%fused_computation.7 | convolution fusion | flops 9664462848 | bytes 10485760 | tf_op jit(solution)/shard_map/wja,ij->awi/dot_general | solution.py:43
  277.7 0.7 compare_reduce_fusion
  278.4 0.1 reshape.50
  278.5 7.1 %gather_fusion.2 = f32[12,256,256]{2,1,0:T(8,128)} fusion(f32[3,16,256,256]{3,2,1,0:T(8,128)} %bitcast.44, s32[12]{0:T(128)S(1)} %reshape.50), kind=kCustom, calls=%fused_computation.2 | custom fusion | bytes 6291552 | tf_op jit(solution)/shard_map/gather | solution.py:16
  285.6 3.4 bitcast_select_fusion
  289.0 74.0 %reduce-scatter.2.cloned.1.call-done = f32[16,3,1024]{2,0,1:T(8,128)} async-done(((f32[256,3,1024]{2,0,1:T(8,128)}), f32[16,3,1024]{2,0,1:T(8,128)}) %reduce-scatter.2.cloned.1.call-update) | async-done | bytes 196624 | tf_op jit(solution)/shard_map/reduce_scatter | solution.py:42
  363.0 0.9 broadcast_multiply_fusion
  363.9 3.7 convolution_bitcast_fusion
  367.6 34.9 %all-gather = f32[256,3,256]{2,0,1:T(8,128)S(1)} all-gather(f32[16,3,256]{2,0,1:T(8,128)S(1)} %convolution_bitcast_fusion), channel_id=2, replica_groups=mesh['pole'=2,'prow'=16,'pcol'=16] {'prow'}, dimensions={0}, use_global_device_ids=true | all-gather | bytes 835584 | tf_op jit(solution)/shard_map/all_gather | solution.py:50
  402.5 0.6 sub.3
  (22 shorter events, 0.4 us)
Async XLA Ops:
  7.2 1.1 copy-start
  7.2 237.9 %all-gather.3.cloned.1.call-start = ((), (), s32[]{:S(2)}) async-start(), calls=%async_computation.1 | async-start | bytes 12632064 | tf_op jit(solution)/shard_map/all_gather | solution.py:34
  9.0 354.0 %reduce-scatter.2.cloned.1.call-start = ((), (), s32[]{:S(2)}) async-start(), calls=%async_computation.2 | async-start | bytes 3342336 | tf_op jit(solution)/shard_map/reduce_scatter | solution.py:42
  252.1 3.1 copy-start.1
  289.0 113.6 %copy-start.3 = (f32[16,3,256]{2,0,1:T(8,128)S(1)}, f32[16,3,256]{2,0,1:T(8,128)}, u32[]{:S(2)}) copy-start(f32[16,3,256]{2,0,1:T(8,128)} %param.7) | copy-start | bytes 147460
  363.9 39.3 %copy-start.2 = (f32[16,3,1024]{2,0,1:T(8,128)}, f32[16,3,1024]{2,0,1:T(8,128)S(1)}, u32[]{:S(2)}) copy-start(f32[16,3,1024]{2,0,1:T(8,128)S(1)} %broadcast_multiply_fusion) | copy-start | bytes 589828
Sparse Core Ops, SparseCore 0:
  13.0 232.0 all-gather.2
  277.7 85.1 reduce-scatter.1

commit v2 on v1

v2 whole, which is shorter than its diff:
```python
import jax
import jax.numpy as jnp
from jax import lax
from jax.sharding import PartitionSpec as P


def diag_product(values, factor):
    return jnp.einsum("awj,wjb->awb", values, factor, precision=lax.Precision.HIGHEST)


def slot_lookup(positions, slots):
    match = positions[:, None, :] == slots[None, :, None]
    return jnp.argmax(match, axis=2), jnp.any(match, axis=2)


def make_shards(prow_size, pcol_size):
    def shards(inverse_trailing, factor_blocks, diag_pivots, structure, owner_map):
        width = factor_blocks.shape[2]
        window = factor_blocks.shape[0]
        local_rows = factor_blocks.shape[1]
        owned = inverse_trailing.shape[0] // width
        row_index = lax.axis_index("prow")
        col_index = lax.axis_index("pcol")
        positions = jnp.take(owner_map, structure, axis=0)
        slots = jnp.arange(owned, dtype=jnp.int32)
        segment = local_rows // pcol_size
        mine = lax.dynamic_slice_in_dim(factor_blocks, col_index * segment, segment, axis=1)
        pieces = lax.all_gather(mine, "prow", axis=1, tiled=True)
        count = pieces.shape[1] // segment
        pieces = pieces.reshape(window, count, segment, width)
        windows = jnp.arange(window)
        dest_slots = jnp.arange(pcol_size, dtype=jnp.int32)[:, None] * owned + slots[None, :]
        dest_index, dest_present = jax.vmap(lambda s: slot_lookup(positions, s))(dest_slots)
        send = pieces[windows[None, :, None], dest_index]
        send = jnp.where(dest_present[..., None, None], send, 0.0)
        send = jnp.transpose(send, (1, 2, 0, 3, 4))
        received = lax.all_to_all(send, "pcol", 2, 2, tiled=True)
        col_factor = received.reshape(window, owned * local_rows, width)
        row_index_map, in_rows = slot_lookup(positions, row_index * owned + slots)
        row_piece = pieces[windows[:, None], row_index_map]
        row_piece = jnp.where(in_rows[..., None, None], row_piece, 0.0)
        row_factor = lax.all_gather(row_piece, "pcol", axis=2, tiled=True)
        row_factor = row_factor.reshape(window, owned * width, width)
        row_mask = jnp.repeat(in_rows.astype(jnp.float32), width, axis=1)
        partial = -jnp.einsum("wja,ij->awi", col_factor, inverse_trailing, precision=lax.Precision.HIGHEST)
        share = partial.shape[0] // pcol_size
        partial = partial.reshape((pcol_size, share) + partial.shape[1:])
        summed = jnp.sum(lax.all_to_all(partial, "pcol", 0, 0, tiled=True), axis=0)
        row_inverse = summed * row_mask[None, :, :]
        local_diag = diag_product(row_inverse, row_factor)
        gathered = lax.all_gather(local_diag, "prow", axis=0, tiled=False)
        total_diag = jnp.sum(gathered, axis=0)
        diag_inverse = diag_pivots - total_diag
        return (row_inverse, diag_inverse)

    return shards


def solution(mesh):
    in_specs = (
        P(("pole", "prow"), "pcol"),
        P("pole", "prow", None),
        P("pcol", "pole", None),
        P(),
        P(),
    )
    out_specs = (P("pcol", "pole", "prow"), P("pcol", "pole", None))
    shards = make_shards(mesh.shape["prow"], mesh.shape["pcol"])
    return jax.shard_map(shards, mesh=mesh, in_specs=in_specs, out_specs=out_specs, check_vma=False)
```

time: 410 us -> 222 us (0.54)
  the two profiles are of different devices: /device:TPU:2 before, /device:TPU:8 now
where the time goes in v2:
time: 222 us
  blocking collectives  76.9 us (35%)
  waiting for transfers between devices  68.4 us (31%)
  matrix products  24.2 us (11%)
  starting transfers between devices  14.7 us (7%)
  between operations  14.2 us (6%)
  local copies, waits for them, and re-layouts  11.8 us (5%)
  other arithmetic  11.6 us (5%)
    all_gather x1, blocking collectives, shards(): pieces = lax.all_gather(mine, 'prow', axis=1, tiled=True)  40.1 us
    all_gather x1, blocking collectives, shards(): gathered = lax.all_gather(local_diag, 'prow', axis=0, tiled=False)  36.8 us
    all_to_all x1, waiting for transfers between devices, shards(): summed = jnp.sum(lax.all_to_all(partial, 'pcol', 0, 0, tiled=True), axis=0)  36.4 us
    all_to_all x1, waiting for transfers between devices, shards(): received = lax.all_to_all(send, 'pcol', 2, 2, tiled=True)  32 us
    dot_general x1, matrix products, shards(): jnp.einsum('wja,ij->awi', col_factor, inverse_trailing, precision=lax.Pre...  20.5 us
    all_to_all x1, starting transfers between devices, shards(): received = lax.all_to_all(send, 'pcol', 2, 2, tiled=True)  7.39 us
    all_to_all x1, starting transfers between devices, shards(): summed = jnp.sum(lax.all_to_all(partial, 'pcol', 0, 0, tiled=True), axis=0)  7.27 us
  transfers between devices with their start and end apart: 3, of which 2 were waited for; matrix products, arithmetic and copies ran while one was open for 13% of the time, Pallas kernels for 0%

profile of v2, /device:TPU:8, one launch (start us, length us, event | category | flops | bytes accessed | tf_op | source)
XLA Modules:
  0.0 221.9 jit_solution(1182232790215958172)
XLA Ops:
  7.2 0.8 compare_select_fusion.2
  8.0 1.4 gather_fusion
  9.6 0.7 and_select_fusion
  10.3 1.2 compare_reduce_fusion
  11.4 0.4 compare_reduce_fusion.1
  11.8 40.1 %all_gather.12 = f32[3,256,256]{2,1,0:T(8,128)S(1)} all-gather(f32[3,16,256]{2,1,0:T(8,128)S(1)} %constant_dynamic-slice_fusion), channel_id=1, replica_groups=mesh['pole'=2,'prow'=16,'pcol'=16] {'prow'}, dimensions={1}, use_global_device_ids=true | all-gather | bytes 835584 | tf_op jit(solution)/shard_map/all_gather | solution.py:28
  52.3 3.9 %gather_fusion.1 = f32[192,16,256]{2,1,0:T(8,128)} fusion(f32[3,16,16,256]{3,2,1,0:T(8,128)S(1)} %bitcast.37, s32[192]{0:T(256)S(1)} %reshape.79), kind=kCustom, calls=%fused_computation.1 | custom fusion | bytes 6292992 | tf_op jit(solution)/shard_map/gather | solution.py:34
  56.2 3.9 %broadcast_select_fusion = f32[3,4,16,16,256]{4,3,1,0,2:T(8,128)} fusion(f32[3,4,16,16,256]{4,3,1,0,2:T(8,128)} %bitcast.39, pred[3,4,16]{1,0,2:T(4,128)(4,1)S(1)} %copy.20), kind=kLoop, calls=%fused_computation.6 | loop fusion | flops 786432 | bytes 6291648 | tf_op jit(solution)/shard_map/jit(_where)/select_n | solution.py:35
  60.1 7.4 %all-to-all-start = ((f32[3,4,16,16,256]{4,3,1,0,2:T(8,128)}), f32[3,4,16,16,256]{4,3,1,0,2:T(8,128)}, u32[]{:S(2)}, u32[]{:S(2)}) async-start(f32[3,4,16,16,256]{4,3,1,0,2:T(8,128)} %broadcast_select_fusion), calls=%async_computation | async-start | bytes 6291456 | tf_op jit(solution)/shard_map/all_to_all | solution.py:37
  67.6 0.9 compare_reduce_fusion.2
  68.6 0.6 gather_fusion.2
  69.2 0.2 compare_reduce_fusion.3
  69.4 0.8 broadcast_select_fusion.1
  70.2 32.0 %all-to-all-done = f32[3,4,16,16,256]{4,3,1,0,2:T(8,128)} async-done(((f32[3,4,16,16,256]{4,3,1,0,2:T(8,128)}), f32[3,4,16,16,256]{4,3,1,0,2:T(8,128)}, u32[]{:S(2)}, u32[]{:S(2)}) %all-to-all-start) | async-done | bytes 3145760 | tf_op jit(solution)/shard_map/all_to_all | solution.py:37
  102.2 2.4 %copy.22 = f32[3,4,16,16,256]{4,3,2,1,0:T(8,128)S(1)} copy(f32[3,4,16,16,256]{4,3,1,0,2:T(8,128)} %all-to-all-done) | data formatting | bytes 6291456 | tf_op jit(solution)/shard_map/all_to_all | solution.py:37
  104.6 0.8 copy-done.1
  105.3 20.5 %fusion.2 = f32[3,256,1024]{2,1,0:T(8,128)S(1)} fusion(f32[3,1024,256]{2,1,0:T(8,128)S(1)} %bitcast.40, f32[1024,1024]{1,0:T(8,128)S(1)} %copy-done.1), kind=kOutput, calls=%fused_computation.5 | convolution fusion | flops 9664462848 | bytes 10485760 | tf_op jit(solution)/shard_map/wja,ij->awi/dot_general | solution.py:45
  125.9 2.1 copy.24
  127.9 7.3 %all-to-all-start.1 = ((f32[16,16,3,1024]{3,1,2,0:T(8,128)}), f32[16,16,3,1024]{3,1,2,0:T(8,128)}, u32[]{:S(2)}, u32[]{:S(2)}) async-start(f32[16,16,3,1024]{3,1,2,0:T(8,128)} %copy.24), calls=%async_computation.1 | async-start | bytes 6291456 | tf_op jit(solution)/shard_map/all_to_all | solution.py:48
  135.3 36.4 %all-to-all-done.1 = f32[16,16,3,1024]{3,1,2,0:T(8,128)} async-done(((f32[16,16,3,1024]{3,1,2,0:T(8,128)}), f32[16,16,3,1024]{3,1,2,0:T(8,128)}, u32[]{:S(2)}, u32[]{:S(2)}) %all-to-all-start.1) | async-done | bytes 3145760 | tf_op jit(solution)/shard_map/all_to_all | solution.py:48
  171.7 2.1 reduce_sum.18
  173.9 3.7 %convolution_bitcast_fusion = f32[16,3,256]{2,0,1:T(8,128)S(1)} fusion(f32[3,1024,256]{2,1,0:T(8,128)} %bitcast.42, f32[16,3,1024]{2,0,1:T(8,128)S(1)} %broadcast_multiply_fusion), kind=kOutput, calls=%fused_computation.7 | convolution fusion | flops 150994944 | bytes 3391488 | tf_op jit(solution)/shard_map/awj,wjb->awb/dot_general | solution.py:8
  177.6 36.8 %all-gather = f32[256,3,256]{2,0,1:T(8,128)S(1)} all-gather(f32[16,3,256]{2,0,1:T(8,128)S(1)} %convolution_bitcast_fusion), channel_id=2, replica_groups=mesh['pole'=2,'prow'=16,'pcol'=16] {'prow'}, dimensions={0}, use_global_device_ids=true | all-gather | bytes 835584 | tf_op jit(solution)/shard_map/all_gather | solution.py:51
  214.4 0.6 sub.3
  (28 shorter events, 0.9 us)
Async XLA Ops:
  7.2 4.6 %copy-start = (f32[3,256,256]{2,1,0:T(8,128)S(1)}, f32[3,256,256]{2,1,0:T(8,128)}, u32[]{:S(2)}) copy-start(f32[3,256,256]{2,1,0:T(8,128)} %param.6) | copy-start | bytes 2359300
  60.1 42.1 %all-to-all-start = ((f32[3,4,16,16,256]{4,3,1,0,2:T(8,128)}), f32[3,4,16,16,256]{4,3,1,0,2:T(8,128)}, u32[]{:S(2)}, u32[]{:S(2)}) async-start(f32[3,4,16,16,256]{4,3,1,0,2:T(8,128)} %broadcast_select_fusion), calls=%async_computation | async-start | bytes 6291456 | tf_op jit(solution)/shard_map/all_to_all | solution.py:37
  67.5 106.4 %all-gather.3.cloned.1.call-start = ((), (), s32[]{:S(2)}) async-start(), calls=%async_computation.2 | async-start | bytes 3342336 | tf_op jit(solution)/shard_map/all_gather | solution.py:42
  102.2 3.1 %copy-start.1 = (f32[1024,1024]{1,0:T(8,128)S(1)}, f32[1024,1024]{1,0:T(8,128)}, u32[]{:S(2)}) copy-start(f32[1024,1024]{1,0:T(8,128)} %param.5) | copy-start | bytes 12582916
  127.9 43.8 %all-to-all-start.1 = ((f32[16,16,3,1024]{3,1,2,0:T(8,128)}), f32[16,16,3,1024]{3,1,2,0:T(8,128)}, u32[]{:S(2)}, u32[]{:S(2)}) async-start(f32[16,16,3,1024]{3,1,2,0:T(8,128)} %copy.24), calls=%async_computation.1 | async-start | bytes 6291456 | tf_op jit(solution)/shard_map/all_to_all | solution.py:48
  173.8 40.6 %copy-start.3 = (f32[16,3,256]{2,0,1:T(8,128)S(1)}, f32[16,3,256]{2,0,1:T(8,128)}, u32[]{:S(2)}) copy-start(f32[16,3,256]{2,0,1:T(8,128)} %param.7) | copy-start | bytes 147460
  173.8 41.2 %copy-start.2 = (f32[16,3,1024]{2,0,1:T(8,128)}, f32[16,3,1024]{2,0,1:T(8,128)S(1)}, u32[]{:S(2)}) copy-start(f32[16,3,1024]{2,0,1:T(8,128)S(1)} %broadcast_multiply_fusion) | copy-start | bytes 589828
Sparse Core Ops, SparseCore 0:
  71.4 69.3 all-gather.2

commit v3 on v2

--- a/solution.py
+++ b/solution.py
@@ -13,6 +13,26 @@
     return jnp.argmax(match, axis=2), jnp.any(match, axis=2)
 
 
+def butterfly_gather(x, axis_name, size):
+    index = lax.axis_index(axis_name)
+    held = x[None]
+    step = 1
+    while step < size:
+        other = lax.ppermute(held, axis_name, perm=[(i, i ^ step) for i in range(size)])
+        lower = (index & step) == 0
+        held = jnp.where(lower, jnp.concatenate([held, other], 0), jnp.concatenate([other, held], 0))
+        step *= 2
+    return held
+
+
+def butterfly_sum(x, axis_name, size):
+    step = 1
+    while step < size:
+        x = x + lax.ppermute(x, axis_name, perm=[(i, i ^ step) for i in range(size)])
+        step *= 2
+    return x
+
+
 def make_shards(prow_size, pcol_size):
     def shards(inverse_trailing, factor_blocks, diag_pivots, structure, owner_map):
         width = factor_blocks.shape[2]
@@ -25,9 +45,8 @@
         slots = jnp.arange(owned, dtype=jnp.int32)
         segment = local_rows // pcol_size
         mine = lax.dynamic_slice_in_dim(factor_blocks, col_index * segment, segment, axis=1)
-        pieces = lax.all_gather(mine, "prow", axis=1, tiled=True)
-        count = pieces.shape[1] // segment
-        pieces = pieces.reshape(window, count, segment, width)
+        pieces = butterfly_gather(mine, "prow", prow_size)
+        pieces = jnp.transpose(pieces, (1, 0, 2, 3))
         windows = jnp.arange(window)
         dest_slots = jnp.arange(pcol_size, dtype=jnp.int32)[:, None] * owned + slots[None, :]
         dest_index, dest_present = jax.vmap(lambda s: slot_lookup(positions, s))(dest_slots)
@@ -48,8 +67,7 @@
         summed = jnp.sum(lax.all_to_all(partial, "pcol", 0, 0, tiled=True), axis=0)
         row_inverse = summed * row_mask[None, :, :]
         local_diag = diag_product(row_inverse, row_factor)
-        gathered = lax.all_gather(local_diag, "prow", axis=0, tiled=False)
-        total_diag = jnp.sum(gathered, axis=0)
+        total_diag = butterfly_sum(local_diag, "prow", prow_size)
         diag_inverse = diag_pivots - total_diag
         return (row_inverse, diag_inverse)
 

time: 222 us -> 283 us (1.27)
  blocking collectives: 76.9 us -> 0 us
  waiting for transfers between devices: 68.4 us -> 145 us
  starting transfers between devices: 14.7 us -> 74 us
    all_gather x2 -> x0, blocking collectives: 76.9 us -> none  [the longest x1 40.1 us: shards(): pieces = lax.all_gather(mine, 'prow', axis=1, tiled=True)]
    ppermute x0 -> x8, waiting for transfers between devices: none -> 63.2 us  [the longest x4 42.8 us: butterfly_gather(): lax.ppermute(held, axis_name, perm=[(i, i ^ step) for i in range(size)])]
    ppermute x0 -> x8, starting transfers between devices: none -> 58.6 us  [the longest x4 40.7 us: butterfly_gather(): lax.ppermute(held, axis_name, perm=[(i, i ^ step) for i in range(size)])]
    all_to_all x1, waiting for transfers between devices: 32 us -> 41.3 us  [shards(): received = lax.all_to_all(send, 'pcol', 2, 2, tiled=True)]
    all_to_all x1, waiting for transfers between devices: 36.4 us -> 40.4 us  [shards(): summed = jnp.sum(lax.all_to_all(partial, 'pcol', 0, 0, tiled=True), axis=0)]
  transfers between devices with their start and end apart: 3 -> 11, of which waited for: 2 -> 9; matrix products, arithmetic and copies ran while one was open for 13% -> 12% of each run, Pallas kernels for 0% -> 0%
where the time goes in v3:
time: 283 us; the launch traced here: 282 us
  waiting for transfers between devices  145 us (51%)
  starting transfers between devices  74 us (26%)
  matrix products  24.2 us (9%)
  between operations  14.2 us (5%)
  local copies, waits for them, and re-layouts  12.9 us (5%)
  other arithmetic  11.7 us (4%)
    ppermute x4, waiting for transfers between devices, butterfly_gather(): lax.ppermute(held, axis_name, perm=[(i, i ^ step) for i in range(size)])  42.8 us
    all_to_all x1, waiting for transfers between devices, shards(): received = lax.all_to_all(send, 'pcol', 2, 2, tiled=True)  41.3 us
    ppermute x4, starting transfers between devices, butterfly_gather(): lax.ppermute(held, axis_name, perm=[(i, i ^ step) for i in range(size)])  40.7 us
    all_to_all x1, waiting for transfers between devices, shards(): summed = jnp.sum(lax.all_to_all(partial, 'pcol', 0, 0, tiled=True), axis=0)  40.4 us
    dot_general x1, matrix products, shards(): jnp.einsum('wja,ij->awi', col_factor, inverse_trailing, precision=lax.Pre...  20.5 us
    ppermute x4, waiting for transfers between devices, butterfly_sum(): lax.ppermute(x, axis_name, perm=[(i, i ^ step) for i in range(size)])  20.5 us
    ppermute x4, starting transfers between devices, butterfly_sum(): lax.ppermute(x, axis_name, perm=[(i, i ^ step) for i in range(size)])  18 us
    all_to_all x1, starting transfers between devices, shards(): summed = jnp.sum(lax.all_to_all(partial, 'pcol', 0, 0, tiled=True), axis=0)  7.98 us
  transfers between devices with their start and end apart: 11, of which 9 were waited for; matrix products, arithmetic and copies ran while one was open for 12% of the time, Pallas kernels for 0%

profile of v3, /device:TPU:8, one launch (start us, length us, event | category | flops | bytes accessed | tf_op | source)
XLA Modules:
  0.0 282.0 jit_solution(11524162687356857849)
XLA Ops:
  8.3 3.8 %collective-permute-start = (f32[1,3,16,256]{3,2,1,0:T(8,128)S(1)}, f32[1,3,16,256]{3,2,1,0:T(8,128)S(1)}, u32[]{:S(2)}, u32[]{:S(2)}) collective-permute-start(f32[1,3,16,256]{3,2,1,0:T(8,128)S(1)} %dynamic-slice_bitcast_fusion), channel_id=1, source_target_pairs={{0,16},{16,0},{32,48},{48,32},{64,80},{80,64},{96,112},{112,96},{1... | collective-permute-start | bytes 147464 | tf_op jit(solution)/shard_map/ppermute | solution.py:21
  15.1 5.2 %collective-permute-start.1 = (f32[2,3,16,256]{3,2,1,0:T(8,128)S(1)}, f32[2,3,16,256]{3,2,1,0:T(8,128)S(1)}, u32[]{:S(2)}, u32[]{:S(2)}) collective-permute-start(f32[2,3,16,256]{3,2,1,0:T(8,128)S(1)} %maximum_select_fusion.3), channel_id=1, source_target_pairs={{0,32},{16,48},{32,0},{48,16},{64,96},{80,112},{96,64},{112,80},{1... | collective-permute-start | bytes 294920 | tf_op jit(solution)/shard_map/ppermute | solution.py:21
  20.3 4.3 %collective-permute-done.1 = f32[2,3,16,256]{3,2,1,0:T(8,128)S(1)} collective-permute-done((f32[2,3,16,256]{3,2,1,0:T(8,128)S(1)}, f32[2,3,16,256]{3,2,1,0:T(8,128)S(1)}, u32[]{:S(2)}, u32[]{:S(2)}) %collective-permute-start.1) | collective-permute-done | bytes 98336 | tf_op jit(solution)/shard_map/ppermute | solution.py:21
  24.7 9.1 %collective-permute-start.2 = (f32[4,3,16,256]{3,2,1,0:T(8,128)S(1)}, f32[4,3,16,256]{3,2,1,0:T(8,128)S(1)}, u32[]{:S(2)}, u32[]{:S(2)}) collective-permute-start(f32[4,3,16,256]{3,2,1,0:T(8,128)S(1)} %maximum_select_fusion.2), channel_id=1, source_target_pairs={{0,64},{16,80},{32,96},{48,112},{64,0},{80,16},{96,32},{112,48},{1... | collective-permute-start | bytes 589832 | tf_op jit(solution)/shard_map/ppermute | solution.py:21
  33.8 14.4 %collective-permute-done.2 = f32[4,3,16,256]{3,2,1,0:T(8,128)S(1)} collective-permute-done((f32[4,3,16,256]{3,2,1,0:T(8,128)S(1)}, f32[4,3,16,256]{3,2,1,0:T(8,128)S(1)}, u32[]{:S(2)}, u32[]{:S(2)}) %collective-permute-start.2) | collective-permute-done | bytes 196640 | tf_op jit(solution)/shard_map/ppermute | solution.py:21
  48.3 22.6 %collective-permute-start.3 = (f32[8,3,16,256]{3,2,1,0:T(8,128)S(1)}, f32[8,3,16,256]{3,2,1,0:T(8,128)S(1)}, u32[]{:S(2)}, u32[]{:S(2)}) collective-permute-start(f32[8,3,16,256]{3,2,1,0:T(8,128)S(1)} %maximum_select_fusion.1), channel_id=1, source_target_pairs={{0,128},{16,144},{32,160},{48,176},{64,192},{80,208},{96,224},{112... | collective-permute-start | bytes 1179656 | tf_op jit(solution)/shard_map/ppermute | solution.py:21
  72.7 24.0 %collective-permute-done.3 = f32[8,3,16,256]{3,2,1,0:T(8,128)S(1)} collective-permute-done((f32[8,3,16,256]{3,2,1,0:T(8,128)S(1)}, f32[8,3,16,256]{3,2,1,0:T(8,128)S(1)}, u32[]{:S(2)}, u32[]{:S(2)}) %collective-permute-start.3) | collective-permute-done | bytes 393248 | tf_op jit(solution)/shard_map/ppermute | solution.py:21
  96.8 3.9 %gather_fusion.1 = f32[192,16,256]{2,1,0:T(8,128)} fusion(f32[3,16,16,256]{3,2,0,1:T(8,128)S(1)} %fusion.5, s32[192]{0:T(256)S(1)} %reshape.75), kind=kCustom, calls=%fused_computation.1 | custom fusion | bytes 6292992 | tf_op jit(solution)/shard_map/gather | solution.py:53
  100.7 3.9 %broadcast_select_fusion = f32[3,4,16,16,256]{4,3,1,0,2:T(8,128)} fusion(f32[3,4,16,16,256]{4,3,1,0,2:T(8,128)} %bitcast.39, pred[3,4,16]{1,0,2:T(4,128)(4,1)S(1)} %copy.20), kind=kLoop, calls=%fused_computation.6 | loop fusion | flops 786432 | bytes 6291648 | tf_op jit(solution)/shard_map/jit(_where)/select_n | solution.py:54
  104.6 7.4 %all-to-all-start = ((f32[3,4,16,16,256]{4,3,1,0,2:T(8,128)}), f32[3,4,16,16,256]{4,3,1,0,2:T(8,128)}, u32[]{:S(2)}, u32[]{:S(2)}) async-start(f32[3,4,16,16,256]{4,3,1,0,2:T(8,128)} %broadcast_select_fusion), calls=%async_computation | async-start | bytes 6291456 | tf_op jit(solution)/shard_map/all_to_all | solution.py:56
  114.7 41.3 %all-to-all-done = f32[3,4,16,16,256]{4,3,1,0,2:T(8,128)} async-done(((f32[3,4,16,16,256]{4,3,1,0,2:T(8,128)}), f32[3,4,16,16,256]{4,3,1,0,2:T(8,128)}, u32[]{:S(2)}, u32[]{:S(2)}) %all-to-all-start) | async-done | bytes 3145760 | tf_op jit(solution)/shard_map/all_to_all | solution.py:56
  156.0 2.4 copy.22
  159.1 20.5 %fusion.2 = f32[3,256,1024]{2,1,0:T(8,128)S(1)} fusion(f32[3,1024,256]{2,1,0:T(8,128)S(1)} %bitcast.40, f32[1024,1024]{1,0:T(8,128)S(1)} %copy-done.1), kind=kOutput, calls=%fused_computation.5 | convolution fusion | flops 9664462848 | bytes 10485760 | tf_op jit(solution)/shard_map/wja,ij->awi/dot_general | solution.py:64
  179.7 2.1 copy.24
  181.8 8.0 %all-to-all-start.1 = ((f32[16,16,3,1024]{3,1,2,0:T(8,128)}), f32[16,16,3,1024]{3,1,2,0:T(8,128)}, u32[]{:S(2)}, u32[]{:S(2)}) async-start(f32[16,16,3,1024]{3,1,2,0:T(8,128)} %copy.24), calls=%async_computation.1 | async-start | bytes 6291456 | tf_op jit(solution)/shard_map/all_to_all | solution.py:67
  189.8 40.4 %all-to-all-done.1 = f32[16,16,3,1024]{3,1,2,0:T(8,128)} async-done(((f32[16,16,3,1024]{3,1,2,0:T(8,128)}), f32[16,16,3,1024]{3,1,2,0:T(8,128)}, u32[]{:S(2)}, u32[]{:S(2)}) %all-to-all-start.1) | async-done | bytes 3145760 | tf_op jit(solution)/shard_map/all_to_all | solution.py:67
  230.2 2.1 reduce_sum.9
  232.4 3.7 %convolution_bitcast_fusion = f32[16,3,256]{2,0,1:T(8,128)S(1)} fusion(f32[3,1024,256]{2,1,0:T(8,128)} %bitcast.42, f32[16,3,1024]{2,0,1:T(8,128)S(1)} %broadcast_multiply_fusion), kind=kOutput, calls=%fused_computation.7 | convolution fusion | flops 150994944 | bytes 3391488 | tf_op jit(solution)/shard_map/awj,wjb->awb/dot_general | solution.py:8
  238.0 4.1 %collective-permute-done.4 = f32[16,3,256]{2,0,1:T(8,128)S(1)} collective-permute-done((f32[16,3,256]{2,0,1:T(8,128)S(1)}, f32[16,3,256]{2,0,1:T(8,128)S(1)}, u32[]{:S(2)}, u32[]{:S(2)}) %collective-permute-start.4) | collective-permute-done | bytes 49184 | tf_op jit(solution)/shard_map/ppermute | solution.py:31
  243.9 5.0 %collective-permute-done.5 = f32[16,3,256]{2,0,1:T(8,128)S(1)} collective-permute-done((f32[16,3,256]{2,0,1:T(8,128)S(1)}, f32[16,3,256]{2,0,1:T(8,128)S(1)}, u32[]{:S(2)}, u32[]{:S(2)}) %collective-permute-start.5) | collective-permute-done | bytes 49184 | tf_op jit(solution)/shard_map/ppermute | solution.py:31
  248.9 3.8 %collective-permute-start.6 = (f32[16,3,256]{2,0,1:T(8,128)S(1)}, f32[16,3,256]{2,0,1:T(8,128)S(1)}, u32[]{:S(2)}, u32[]{:S(2)}) collective-permute-start(f32[16,3,256]{2,0,1:T(8,128)S(1)} %add.73), channel_id=1, source_target_pairs={{0,64},{16,80},{32,96},{48,112},{64,0},{80,16},{96,32},{112,48},{1... | collective-permute-start | bytes 147464 | tf_op jit(solution)/shard_map/ppermute | solution.py:31
  252.8 6.9 %collective-permute-done.6 = f32[16,3,256]{2,0,1:T(8,128)S(1)} collective-permute-done((f32[16,3,256]{2,0,1:T(8,128)S(1)}, f32[16,3,256]{2,0,1:T(8,128)S(1)}, u32[]{:S(2)}, u32[]{:S(2)}) %collective-permute-start.6) | collective-permute-done | bytes 49184 | tf_op jit(solution)/shard_map/ppermute | solution.py:31
  259.7 10.3 %collective-permute-start.7 = (f32[16,3,256]{2,0,1:T(8,128)S(1)}, f32[16,3,256]{2,0,1:T(8,128)S(1)}, u32[]{:S(2)}, u32[]{:S(2)}) collective-permute-start(f32[16,3,256]{2,0,1:T(8,128)S(1)} %add.74), channel_id=1, source_target_pairs={{0,128},{16,144},{32,160},{48,176},{64,192},{80,208},{96,224},{112... | collective-permute-start | bytes 147464 | tf_op jit(solution)/shard_map/ppermute | solution.py:31
  270.0 4.6 %collective-permute-done.7 = f32[16,3,256]{2,0,1:T(8,128)S(1)} collective-permute-done((f32[16,3,256]{2,0,1:T(8,128)S(1)}, f32[16,3,256]{2,0,1:T(8,128)S(1)}, u32[]{:S(2)}, u32[]{:S(2)}) %collective-permute-start.7) | collective-permute-done | bytes 49184 | tf_op jit(solution)/shard_map/ppermute | solution.py:31
  (48 shorter events, 14.2 us)
Async XLA Ops:
  7.2 1.1 copy-start
  8.3 6.8 %collective-permute-start = (f32[1,3,16,256]{3,2,1,0:T(8,128)S(1)}, f32[1,3,16,256]{3,2,1,0:T(8,128)S(1)}, u32[]{:S(2)}, u32[]{:S(2)}) collective-permute-start(f32[1,3,16,256]{3,2,1,0:T(8,128)S(1)} %dynamic-slice_bitcast_fusion), channel_id=1, source_target_pairs={{0,16},{16,0},{32,48},{48,32},{64,80},{80,64},{96,112},{112,96},{1... | collective-permute-start | bytes 147464 | tf_op jit(solution)/shard_map/ppermute | solution.py:21
  15.1 9.5 %collective-permute-start.1 = (f32[2,3,16,256]{3,2,1,0:T(8,128)S(1)}, f32[2,3,16,256]{3,2,1,0:T(8,128)S(1)}, u32[]{:S(2)}, u32[]{:S(2)}) collective-permute-start(f32[2,3,16,256]{3,2,1,0:T(8,128)S(1)} %maximum_select_fusion.3), channel_id=1, source_target_pairs={{0,32},{16,48},{32,0},{48,16},{64,96},{80,112},{96,64},{112,80},{1... | collective-permute-start | bytes 294920 | tf_op jit(solution)/shard_map/ppermute | solution.py:21
  24.7 23.5 %collective-permute-start.2 = (f32[4,3,16,256]{3,2,1,0:T(8,128)S(1)}, f32[4,3,16,256]{3,2,1,0:T(8,128)S(1)}, u32[]{:S(2)}, u32[]{:S(2)}) collective-permute-start(f32[4,3,16,256]{3,2,1,0:T(8,128)S(1)} %maximum_select_fusion.2), channel_id=1, source_target_pairs={{0,64},{16,80},{32,96},{48,112},{64,0},{80,16},{96,32},{112,48},{1... | collective-permute-start | bytes 589832 | tf_op jit(solution)/shard_map/ppermute | solution.py:21
  48.3 48.5 %collective-permute-start.3 = (f32[8,3,16,256]{3,2,1,0:T(8,128)S(1)}, f32[8,3,16,256]{3,2,1,0:T(8,128)S(1)}, u32[]{:S(2)}, u32[]{:S(2)}) collective-permute-start(f32[8,3,16,256]{3,2,1,0:T(8,128)S(1)} %maximum_select_fusion.1), channel_id=1, source_target_pairs={{0,128},{16,144},{32,160},{48,176},{64,192},{80,208},{96,224},{112... | collective-permute-start | bytes 1179656 | tf_op jit(solution)/shard_map/ppermute | solution.py:21
  104.6 51.4 %all-to-all-start = ((f32[3,4,16,16,256]{4,3,1,0,2:T(8,128)}), f32[3,4,16,16,256]{4,3,1,0,2:T(8,128)}, u32[]{:S(2)}, u32[]{:S(2)}) async-start(f32[3,4,16,16,256]{4,3,1,0,2:T(8,128)} %broadcast_select_fusion), calls=%async_computation | async-start | bytes 6291456 | tf_op jit(solution)/shard_map/all_to_all | solution.py:56
  112.0 120.4 %all-gather.2.cloned.1.call-start = ((), (), s32[]{:S(2)}) async-start(), calls=%async_computation.2 | async-start | bytes 3342336 | tf_op jit(solution)/shard_map/all_gather | solution.py:61
  156.0 3.1 %copy-start.1 = (f32[1024,1024]{1,0:T(8,128)S(1)}, f32[1024,1024]{1,0:T(8,128)}, u32[]{:S(2)}) copy-start(f32[1024,1024]{1,0:T(8,128)} %param.5) | copy-start | bytes 12582916
  181.8 48.4 %all-to-all-start.1 = ((f32[16,16,3,1024]{3,1,2,0:T(8,128)}), f32[16,16,3,1024]{3,1,2,0:T(8,128)}, u32[]{:S(2)}, u32[]{:S(2)}) async-start(f32[16,16,3,1024]{3,1,2,0:T(8,128)} %copy.24), calls=%async_computation.1 | async-start | bytes 6291456 | tf_op jit(solution)/shard_map/all_to_all | solution.py:67
  189.8 84.7 %copy-start.3 = (f32[16,3,256]{2,0,1:T(8,128)S(1)}, f32[16,3,256]{2,0,1:T(8,128)}, u32[]{:S(2)}) copy-start(f32[16,3,256]{2,0,1:T(8,128)} %param.7) | copy-start | bytes 147460
  232.3 42.9 %copy-start.2 = (f32[16,3,1024]{2,0,1:T(8,128)}, f32[16,3,1024]{2,0,1:T(8,128)S(1)}, u32[]{:S(2)}) copy-start(f32[16,3,1024]{2,0,1:T(8,128)S(1)} %broadcast_multiply_fusion) | copy-start | bytes 589828
  236.0 6.0 %collective-permute-start.4 = (f32[16,3,256]{2,0,1:T(8,128)S(1)}, f32[16,3,256]{2,0,1:T(8,128)S(1)}, u32[]{:S(2)}, u32[]{:S(2)}) collective-permute-start(f32[16,3,256]{2,0,1:T(8,128)S(1)} %convolution_bitcast_fusion), channel_id=1, source_target_pairs={{0,16},{16,0},{32,48},{48,32},{64,80},{80,64},{96,112},{112,96},{1... | collective-permute-start | bytes 147464 | tf_op jit(solution)/shard_map/ppermute | solution.py:31
  242.0 6.9 %collective-permute-start.5 = (f32[16,3,256]{2,0,1:T(8,128)S(1)}, f32[16,3,256]{2,0,1:T(8,128)S(1)}, u32[]{:S(2)}, u32[]{:S(2)}) collective-permute-start(f32[16,3,256]{2,0,1:T(8,128)S(1)} %add.72), channel_id=1, source_target_pairs={{0,32},{16,48},{32,0},{48,16},{64,96},{80,112},{96,64},{112,80},{1... | collective-permute-start | bytes 147464 | tf_op jit(solution)/shard_map/ppermute | solution.py:31
  248.9 10.7 %collective-permute-start.6 = (f32[16,3,256]{2,0,1:T(8,128)S(1)}, f32[16,3,256]{2,0,1:T(8,128)S(1)}, u32[]{:S(2)}, u32[]{:S(2)}) collective-permute-start(f32[16,3,256]{2,0,1:T(8,128)S(1)} %add.73), channel_id=1, source_target_pairs={{0,64},{16,80},{32,96},{48,112},{64,0},{80,16},{96,32},{112,48},{1... | collective-permute-start | bytes 147464 | tf_op jit(solution)/shard_map/ppermute | solution.py:31
  259.7 14.9 %collective-permute-start.7 = (f32[16,3,256]{2,0,1:T(8,128)S(1)}, f32[16,3,256]{2,0,1:T(8,128)S(1)}, u32[]{:S(2)}, u32[]{:S(2)}) collective-permute-start(f32[16,3,256]{2,0,1:T(8,128)S(1)} %add.74), channel_id=1, source_target_pairs={{0,128},{16,144},{32,160},{48,176},{64,192},{80,208},{96,224},{112... | collective-permute-start | bytes 147464 | tf_op jit(solution)/shard_map/ppermute | solution.py:31
Sparse Core Ops, SparseCore 0:
  115.9 69.9 all-gather.1

commit v4 on v2

--- a/solution.py
+++ b/solution.py
@@ -42,7 +42,7 @@
         row_factor = lax.all_gather(row_piece, "pcol", axis=2, tiled=True)
         row_factor = row_factor.reshape(window, owned * width, width)
         row_mask = jnp.repeat(in_rows.astype(jnp.float32), width, axis=1)
-        partial = -jnp.einsum("wja,ij->awi", col_factor, inverse_trailing, precision=lax.Precision.HIGHEST)
+        partial = -jnp.einsum("wja,ij->awi", col_factor, inverse_trailing, precision=lax.Precision.HIGH)
         share = partial.shape[0] // pcol_size
         partial = partial.reshape((pcol_size, share) + partial.shape[1:])
         summed = jnp.sum(lax.all_to_all(partial, "pcol", 0, 0, tiled=True), axis=0)

time: 222 us -> 220 us (level)
  the two profiles are of different devices: /device:TPU:8 before, /device:TPU:32 now
where the time goes in v4:
time: 220 us; the launch traced here: 219 us
  waiting for transfers between devices  81.7 us (37%)
  blocking collectives  73.5 us (33%)
  between operations  14.2 us (6%)
  matrix products  13.6 us (6%)
  starting transfers between devices  13.1 us (6%)
  local copies, waits for them, and re-layouts  11.7 us (5%)
  other arithmetic  11.5 us (5%)
    all_to_all x1, waiting for transfers between devices, shards(): summed = jnp.sum(lax.all_to_all(partial, 'pcol', 0, 0, tiled=True), axis=0)  48.5 us
    all_gather x1, blocking collectives, shards(): pieces = lax.all_gather(mine, 'prow', axis=1, tiled=True)  37.7 us
    all_gather x1, blocking collectives, shards(): gathered = lax.all_gather(local_diag, 'prow', axis=0, tiled=False)  35.8 us
    all_to_all x1, waiting for transfers between devices, shards(): received = lax.all_to_all(send, 'pcol', 2, 2, tiled=True)  33.2 us
    dot_general x1, matrix products, shards(): jnp.einsum('wja,ij->awi', col_factor, inverse_trailing, precision=lax.Pre...  9.92 us
    all_to_all x1, starting transfers between devices, shards(): received = lax.all_to_all(send, 'pcol', 2, 2, tiled=True)  7.08 us
    all_to_all x1, starting transfers between devices, shards(): summed = jnp.sum(lax.all_to_all(partial, 'pcol', 0, 0, tiled=True), axis=0)  5.76 us
  transfers between devices with their start and end apart: 3, of which 2 were waited for; matrix products, arithmetic and copies ran while one was open for 9% of the time, Pallas kernels for 0%

profile of v4, /device:TPU:32, one launch (start us, length us, event | category | flops | bytes accessed | tf_op | source)
XLA Modules:
  0.0 219.3 jit_solution(12595036205994784785)
XLA Ops:
  7.2 0.8 compare_select_fusion.2
  8.0 1.4 gather_fusion
  9.6 0.7 and_select_fusion
  10.3 1.2 compare_reduce_fusion
  11.4 0.4 compare_reduce_fusion.1
  11.8 37.7 %all_gather.12 = f32[3,256,256]{2,1,0:T(8,128)S(1)} all-gather(f32[3,16,256]{2,1,0:T(8,128)S(1)} %constant_dynamic-slice_fusion), channel_id=1, replica_groups=mesh['pole'=2,'prow'=16,'pcol'=16] {'prow'}, dimensions={1}, use_global_device_ids=true | all-gather | bytes 835584 | tf_op jit(solution)/shard_map/all_gather | solution.py:28
  49.9 3.9 %gather_fusion.1 = f32[192,16,256]{2,1,0:T(8,128)} fusion(f32[3,16,16,256]{3,2,1,0:T(8,128)S(1)} %bitcast.37, s32[192]{0:T(256)S(1)} %reshape.79), kind=kCustom, calls=%fused_computation.1 | custom fusion | bytes 6292992 | tf_op jit(solution)/shard_map/gather | solution.py:34
  53.7 3.9 %broadcast_select_fusion = f32[3,4,16,16,256]{4,3,1,0,2:T(8,128)} fusion(f32[3,4,16,16,256]{4,3,1,0,2:T(8,128)} %bitcast.39, pred[3,4,16]{1,0,2:T(4,128)(4,1)S(1)} %copy.20), kind=kLoop, calls=%fused_computation.6 | loop fusion | flops 786432 | bytes 6291648 | tf_op jit(solution)/shard_map/jit(_where)/select_n | solution.py:35
  57.7 7.1 %all-to-all-start = ((f32[3,4,16,16,256]{4,3,1,0,2:T(8,128)}), f32[3,4,16,16,256]{4,3,1,0,2:T(8,128)}, u32[]{:S(2)}, u32[]{:S(2)}) async-start(f32[3,4,16,16,256]{4,3,1,0,2:T(8,128)} %broadcast_select_fusion), calls=%async_computation | async-start | bytes 6291456 | tf_op jit(solution)/shard_map/all_to_all | solution.py:37
  64.8 0.2 all-gather.3.cloned.1.call-start
  65.0 0.7 compare_reduce_fusion.2
  65.8 0.6 gather_fusion.2
  66.7 0.8 broadcast_select_fusion.1
  67.5 33.2 %all-to-all-done = f32[3,4,16,16,256]{4,3,1,0,2:T(8,128)} async-done(((f32[3,4,16,16,256]{4,3,1,0,2:T(8,128)}), f32[3,4,16,16,256]{4,3,1,0,2:T(8,128)}, u32[]{:S(2)}, u32[]{:S(2)}) %all-to-all-start) | async-done | bytes 3145760 | tf_op jit(solution)/shard_map/all_to_all | solution.py:37
  100.7 2.5 %copy.22 = f32[3,4,16,16,256]{4,3,2,1,0:T(8,128)S(1)} copy(f32[3,4,16,16,256]{4,3,1,0,2:T(8,128)} %all-to-all-done) | data formatting | bytes 6291456 | tf_op jit(solution)/shard_map/all_to_all | solution.py:37
  103.2 0.6 copy-done.1
  103.8 9.9 %fusion.2 = f32[3,256,1024]{2,1,0:T(8,128)S(1)} fusion(f32[3,1024,256]{2,1,0:T(8,128)S(1)} %bitcast.40, f32[1024,1024]{1,0:T(8,128)S(1)} %copy-done.1), kind=kOutput, calls=%fused_computation.5 | convolution fusion | flops 4832624640 | bytes 10485760 | tf_op jit(solution)/shard_map/wja,ij->awi/dot_general | solution.py:45
  113.8 1.9 copy.24
  115.7 5.8 %all-to-all-start.1 = ((f32[16,16,3,1024]{3,1,2,0:T(8,128)}), f32[16,16,3,1024]{3,1,2,0:T(8,128)}, u32[]{:S(2)}, u32[]{:S(2)}) async-start(f32[16,16,3,1024]{3,1,2,0:T(8,128)} %copy.24), calls=%async_computation.1 | async-start | bytes 6291456 | tf_op jit(solution)/shard_map/all_to_all | solution.py:48
  121.5 48.5 %all-to-all-done.1 = f32[16,16,3,1024]{3,1,2,0:T(8,128)} async-done(((f32[16,16,3,1024]{3,1,2,0:T(8,128)}), f32[16,16,3,1024]{3,1,2,0:T(8,128)}, u32[]{:S(2)}, u32[]{:S(2)}) %all-to-all-start.1) | async-done | bytes 3145760 | tf_op jit(solution)/shard_map/all_to_all | solution.py:48
  170.1 2.1 reduce_sum.18
  172.2 3.7 %convolution_bitcast_fusion = f32[16,3,256]{2,0,1:T(8,128)S(1)} fusion(f32[3,1024,256]{2,1,0:T(8,128)} %bitcast.42, f32[16,3,1024]{2,0,1:T(8,128)S(1)} %broadcast_multiply_fusion), kind=kOutput, calls=%fused_computation.7 | convolution fusion | flops 150994944 | bytes 3391488 | tf_op jit(solution)/shard_map/awj,wjb->awb/dot_general | solution.py:8
  175.9 35.8 %all-gather = f32[256,3,256]{2,0,1:T(8,128)S(1)} all-gather(f32[16,3,256]{2,0,1:T(8,128)S(1)} %convolution_bitcast_fusion), channel_id=2, replica_groups=mesh['pole'=2,'prow'=16,'pcol'=16] {'prow'}, dimensions={0}, use_global_device_ids=true | all-gather | bytes 835584 | tf_op jit(solution)/shard_map/all_gather | solution.py:51
  211.8 0.6 sub.3
  (28 shorter events, 1.1 us)
Async XLA Ops:
  7.2 4.6 %copy-start = (f32[3,256,256]{2,1,0:T(8,128)S(1)}, f32[3,256,256]{2,1,0:T(8,128)}, u32[]{:S(2)}) copy-start(f32[3,256,256]{2,1,0:T(8,128)} %param.6) | copy-start | bytes 2359300
  57.7 43.0 %all-to-all-start = ((f32[3,4,16,16,256]{4,3,1,0,2:T(8,128)}), f32[3,4,16,16,256]{4,3,1,0,2:T(8,128)}, u32[]{:S(2)}, u32[]{:S(2)}) async-start(f32[3,4,16,16,256]{4,3,1,0,2:T(8,128)} %broadcast_select_fusion), calls=%async_computation | async-start | bytes 6291456 | tf_op jit(solution)/shard_map/all_to_all | solution.py:37
  64.8 107.5 %all-gather.3.cloned.1.call-start = ((), (), s32[]{:S(2)}) async-start(), calls=%async_computation.2 | async-start | bytes 3342336 | tf_op jit(solution)/shard_map/all_gather | solution.py:42
  100.6 3.2 %copy-start.1 = (f32[1024,1024]{1,0:T(8,128)S(1)}, f32[1024,1024]{1,0:T(8,128)}, u32[]{:S(2)}) copy-start(f32[1024,1024]{1,0:T(8,128)} %param.5) | copy-start | bytes 12582916
  115.7 54.4 %all-to-all-start.1 = ((f32[16,16,3,1024]{3,1,2,0:T(8,128)}), f32[16,16,3,1024]{3,1,2,0:T(8,128)}, u32[]{:S(2)}, u32[]{:S(2)}) async-start(f32[16,16,3,1024]{3,1,2,0:T(8,128)} %copy.24), calls=%async_computation.1 | async-start | bytes 6291456 | tf_op jit(solution)/shard_map/all_to_all | solution.py:48
  172.2 39.7 %copy-start.3 = (f32[16,3,256]{2,0,1:T(8,128)S(1)}, f32[16,3,256]{2,0,1:T(8,128)}, u32[]{:S(2)}) copy-start(f32[16,3,256]{2,0,1:T(8,128)} %param.7) | copy-start | bytes 147460
  172.2 40.3 %copy-start.2 = (f32[16,3,1024]{2,0,1:T(8,128)}, f32[16,3,1024]{2,0,1:T(8,128)S(1)}, u32[]{:S(2)}) copy-start(f32[16,3,1024]{2,0,1:T(8,128)S(1)} %broadcast_multiply_fusion) | copy-start | bytes 589828
Sparse Core Ops, SparseCore 0:
  68.7 99.2 all-gather.2

commit v5 on v2

--- a/solution.py
+++ b/solution.py
@@ -1,3 +1,5 @@
+import functools
+
 import jax
 import jax.numpy as jnp
 from jax import lax
@@ -11,6 +13,16 @@
 def slot_lookup(positions, slots):
     match = positions[:, None, :] == slots[None, :, None]
     return jnp.argmax(match, axis=2), jnp.any(match, axis=2)
+
+
+PACKED = (6, 8, 12)
+
+
+def pack_order(present, size):
+    rank = jnp.cumsum(present.astype(jnp.int32), axis=1) - 1
+    target = jnp.arange(size, dtype=jnp.int32)
+    hit = present[:, None, :] & (rank[:, None, :] == target[None, :, None])
+    return jnp.argmax(hit, axis=2).astype(jnp.int32), jnp.any(hit, axis=2)
 
 
 def make_shards(prow_size, pcol_size):
@@ -29,24 +41,47 @@
         count = pieces.shape[1] // segment
         pieces = pieces.reshape(window, count, segment, width)
         windows = jnp.arange(window)
+        flat_slots = window * owned
         dest_slots = jnp.arange(pcol_size, dtype=jnp.int32)[:, None] * owned + slots[None, :]
         dest_index, dest_present = jax.vmap(lambda s: slot_lookup(positions, s))(dest_slots)
-        send = pieces[windows[None, :, None], dest_index]
-        send = jnp.where(dest_present[..., None, None], send, 0.0)
-        send = jnp.transpose(send, (1, 2, 0, 3, 4))
-        received = lax.all_to_all(send, "pcol", 2, 2, tiled=True)
-        col_factor = received.reshape(window, owned * local_rows, width)
+        dest_index = dest_index.reshape(pcol_size, flat_slots)
+        dest_present = dest_present.reshape(pcol_size, flat_slots)
         row_index_map, in_rows = slot_lookup(positions, row_index * owned + slots)
         row_piece = pieces[windows[:, None], row_index_map]
         row_piece = jnp.where(in_rows[..., None, None], row_piece, 0.0)
         row_factor = lax.all_gather(row_piece, "pcol", axis=2, tiled=True)
         row_factor = row_factor.reshape(window, owned * width, width)
-        row_mask = jnp.repeat(in_rows.astype(jnp.float32), width, axis=1)
+        needed = jnp.max(jnp.sum(dest_present.astype(jnp.int32), axis=1))
+        branch = jnp.sum((needed > jnp.array(PACKED[:-1], jnp.int32)).astype(jnp.int32))
+
+        def route(size, pieces):
+            send_slot, send_valid = pack_order(dest_present, size)
+            send_w = send_slot // owned
+            send_j = jnp.take_along_axis(dest_index, send_slot, axis=1)
+            send = pieces[send_w, send_j]
+            send = jnp.where(send_valid[..., None, None], send, 0.0)
+            received = lax.all_to_all(send, "pcol", 0, 0, tiled=True)
+            blocks = jnp.transpose(received, (1, 0, 2, 3)).reshape(size, local_rows, width)
+            mine = dest_present[col_index]
+            rank = jnp.clip(jnp.cumsum(mine.astype(jnp.int32)) - 1, 0, size - 1)
+            return jnp.where(mine[:, None, None], blocks[rank], 0.0)
+
+        def reduce_rows(size, partial):
+            pair_slot, _ = pack_order(listed[None, :], size)
+            chosen = jnp.take(partial, pair_slot[0], axis=1)
+            share = chosen.shape[0] // pcol_size
+            chosen = chosen.reshape((pcol_size, share) + chosen.shape[1:])
+            summed = jnp.sum(lax.all_to_all(chosen, "pcol", 0, 0, tiled=True), axis=0)
+            pair_rank = jnp.clip(jnp.cumsum(listed.astype(jnp.int32)) - 1, 0, size - 1)
+            return jnp.where(listed[None, :, None], jnp.take(summed, pair_rank, axis=1), 0.0)
+
+        listed = in_rows.reshape(flat_slots)
+        col_factor = lax.switch(branch, [functools.partial(route, size) for size in PACKED], pieces)
+        col_factor = col_factor.reshape(window, owned * local_rows, width)
         partial = -jnp.einsum("wja,ij->awi", col_factor, inverse_trailing, precision=lax.Precision.HIGHEST)
-        share = partial.shape[0] // pcol_size
-        partial = partial.reshape((pcol_size, share) + partial.shape[1:])
-        summed = jnp.sum(lax.all_to_all(partial, "pcol", 0, 0, tiled=True), axis=0)
-        row_inverse = summed * row_mask[None, :, :]
+        partial = partial.reshape(partial.shape[0], flat_slots, width)
+        rows = lax.switch(branch, [functools.partial(reduce_rows, size) for size in PACKED], partial)
+        row_inverse = rows.reshape(rows.shape[0], window, owned * width)
         local_diag = diag_product(row_inverse, row_factor)
         gathered = lax.all_gather(local_diag, "prow", axis=0, tiled=False)
         total_diag = jnp.sum(gathered, axis=0)

time: 222 us -> 207 us (0.932)
  the two profiles are of different devices: /device:TPU:8 before, /device:TPU:32 now
where the time goes in v5:
time: 207 us
  blocking collectives  71.2 us (34%)
  waiting for transfers between devices  44.8 us (22%)
  matrix products  26.5 us (13%)
  local copies, waits for them, and re-layouts  20 us (10%)
  other arithmetic  18.4 us (9%)
  between operations  14.8 us (7%)
  starting transfers between devices  11 us (5%)
    all_gather x1, blocking collectives, shards(): pieces = lax.all_gather(mine, 'prow', axis=1, tiled=True)  37.7 us
    all_gather x1, blocking collectives, shards(): gathered = lax.all_gather(local_diag, 'prow', axis=0, tiled=False)  33.5 us
    all_to_all x1, waiting for transfers between devices, route(): received = lax.all_to_all(send, 'pcol', 0, 0, tiled=True)  24.3 us
    dot_general x1, matrix products, shards(): jnp.einsum('wja,ij->awi', col_factor, inverse_trailing, precision=lax.Pre...  22.8 us
    all_to_all x1, waiting for transfers between devices, reduce_rows(): summed = jnp.sum(lax.all_to_all(chosen, 'pcol', 0, 0, tiled=True), axis=0)  20.5 us
    all_to_all x1, starting transfers between devices, route(): received = lax.all_to_all(send, 'pcol', 0, 0, tiled=True)  7.03 us
  transfers between devices with their start and end apart: 3, of which 2 were waited for; matrix products, arithmetic and copies ran while one was open for 26% of the time, Pallas kernels for 0%

profile of v5, /device:TPU:32, one launch (start us, length us, event | category | flops | bytes accessed | tf_op | source)
XLA Modules:
  0.0 207.0 jit_solution(12471663807410518597)
XLA Ops:
  8.1 1.4 gather_fusion.15
  11.3 37.7 %all_gather.12 = f32[3,256,256]{2,1,0:T(8,128)S(1)} all-gather(f32[3,16,256]{2,1,0:T(8,128)S(1)} %constant_dynamic-slice_fusion), channel_id=1, replica_groups=mesh['pole'=2,'prow'=16,'pcol'=16] {'prow'}, dimensions={1}, use_global_device_ids=true | all-gather | bytes 835584 | tf_op jit(solution)/shard_map/all_gather | solution.py:40
  50.8 1.2 compare_reduce_fusion
  52.7 1.3 fusion.49
  54.6 46.4 %conditional.2 = (f32[3,1024,256]{2,1,0:T(8,128)}) conditional(s32[]{:T(128)} %clamp.64, (pred[16,3,4]{0,2,1:T(4,128)(4,1)S(1)}, s32[]{:T(128)}, s32[16,3,4]{0,2,1:T(4,128)S(1)}, f32[3,16,16,256]{3,2,1,0:T(8,128)S(1)}) %tuple.104, (pred[16,3,4]{0,2,1:T(4,128)(4,1)S(1)}, s32[]{:T(128)}, s32[16,3,4]{0,2,1:T(4,128)S(1)}, ...), branch_computations={%region_6.11_spmd, %region_11.16_spmd, %region_16.21_spmd} | conditional | flops 1610383 | bytes 40940528 | solution.py:79
  55.5 1.3 gather_fusion.5
  58.3 1.6 broadcast_select_fusion.1
  59.9 7.0 %all-to-all-start.1 = ((f32[16,8,16,256]{3,2,1,0:T(8,128)}), f32[16,8,16,256]{3,2,1,0:T(8,128)S(1)}, u32[]{:S(2)}, u32[]{:S(2)}) async-start(f32[16,8,16,256]{3,2,1,0:T(8,128)} %broadcast_select_fusion.1), calls=%async_computation.1 | async-start | bytes 4194304 | tf_op jit(solution)/shard_map/cond/branch_1_fun/all_to_all | solution.py:63
  67.7 24.3 %all-to-all-done.1 = f32[16,8,16,256]{3,2,1,0:T(8,128)S(1)} async-done(((f32[16,8,16,256]{3,2,1,0:T(8,128)}), f32[16,8,16,256]{3,2,1,0:T(8,128)S(1)}, u32[]{:S(2)}, u32[]{:S(2)}) %all-to-all-start.1) | async-done | bytes 2097184 | tf_op jit(solution)/shard_map/cond/branch_1_fun/all_to_all | solution.py:63
  92.0 1.4 copy-done.2
  93.4 1.8 copy.231
  95.2 2.5 %gather_fusion.4 = f32[12,256,256]{2,1,0:T(8,128)} fusion(f32[8,256,256]{2,1,0:T(8,128)S(1)} %bitcast.147, s32[1024]{0:T(1024)S(1)} %pad_clamp_fusion.1), kind=kCustom, calls=%fused_computation.4 | custom fusion | bytes 6291504 | tf_op jit(solution)/shard_map/cond/branch_1_fun/gather | solution.py:67
  97.6 3.4 %bitcast_select_fusion.1 = f32[3,1024,256]{2,1,0:T(8,128)} fusion(pred[3,1024]{1,0:T(4,128)(4,1)S(1)} %bitcast.176, f32[3,1024,256]{2,1,0:T(8,128)} %bitcast.155), kind=kLoop, calls=%fused_computation.46 | loop fusion | flops 786432 | bytes 6294528 | tf_op jit(solution)/shard_map/cond/branch_1_fun/jit(_where)/select_n | solution.py:67
  101.0 22.8 %fusion.42 = f32[256,3,1024]{2,0,1:T(8,128)S(1)} fusion(f32[3,1024,256]{2,1,0:T(8,128)} %get-tuple-element.206, f32[1024,1024]{1,0:T(8,128)} %param.12), kind=kOutput, calls=%fused_computation.162 | convolution fusion | flops 9663676416 | bytes 10485760 | tf_op jit(solution)/shard_map/wja,ij->awi/dot_general | solution.py:81
  123.8 38.4 %conditional.3 = (f32[16,3,1024]{2,0,1:T(8,128)S(1)}) conditional(s32[]{:T(128)} %clamp.64, (pred[3,4]{1,0:T(4,128)(4,1)S(1)}, f32[256,3,1024]{2,0,1:T(8,128)S(1)}) %tuple.49, (pred[3,4]{1,0:T(4,128)(4,1)S(1)}, f32[256,3,1024]{2,0,1:T(8,128)S(1)}) %tuple.49, (pred[3,4]{1,0:T(4,128)(4,1)S(1)}, ...), branch_computations={%region_21.26_spmd, %region_26.31_spmd, %region_31.36_spmd} | conditional | flops 2412092 | bytes 46236924 | solution.py:83
  125.1 2.4 %copy.250 = f32[256,3,1024]{0,2,1:T(8,128)} copy(f32[256,3,1024]{2,0,1:T(8,128)S(1)} %get-tuple-element.188) | data formatting | bytes 6291456 | tf_op jit(solution)/shard_map
  127.5 2.1 %neg.8 = f32[256,3,1024]{0,2,1:T(8,128)S(1)} negate(f32[256,3,1024]{0,2,1:T(8,128)} %copy.250) | non-fusion elementwise | flops 786432 | bytes 6291456 | tf_op jit(solution)/shard_map/neg | solution.py:81
  129.6 2.4 %copy.242 = f32[256,12,256]{2,0,1:T(8,128)} copy(f32[256,12,256]{0,2,1:T(8,128)S(1)} %bitcast.152) | data formatting | bytes 6291456 | tf_op jit(solution)/shard_map/reshape | solution.py:82
  132.0 2.6 %gather_fusion.11 = f32[8,256,256]{2,1,0:T(8,128)S(1)} fusion(f32[256,12,256]{2,0,1:T(8,128)} %copy.242, s32[1024]{0:T(1024)S(1)} %pad_clamp_fusion.6), kind=kCustom, calls=%fused_computation.11 | custom fusion | bytes 4194336 | tf_op jit(solution)/shard_map/cond/branch_1_fun/jit(_take)/gather | solution.py:71
  134.6 1.8 copy_select_fusion.1
  136.3 3.9 %all-to-all-start.4 = ((f32[16,16,8,256]{3,1,2,0:T(8,128)}), f32[16,16,8,256]{3,1,2,0:T(8,128)S(1)}, u32[]{:S(2)}, u32[]{:S(2)}) async-start(f32[16,16,8,256]{3,1,2,0:T(8,128)} %copy_select_fusion.1), calls=%async_computation.4 | async-start | bytes 4194304 | tf_op jit(solution)/shard_map/cond/branch_1_fun/all_to_all | solution.py:74
  140.5 20.5 %all-to-all-done.4 = f32[16,16,8,256]{3,1,2,0:T(8,128)S(1)} async-done(((f32[16,16,8,256]{3,1,2,0:T(8,128)}), f32[16,16,8,256]{3,1,2,0:T(8,128)S(1)}, u32[]{:S(2)}, u32[]{:S(2)}) %all-to-all-start.4) | async-done | bytes 2097184 | tf_op jit(solution)/shard_map/cond/branch_1_fun/all_to_all | solution.py:74
  162.3 3.7 %convolution_bitcast_fusion = f32[16,3,256]{2,0,1:T(8,128)S(1)} fusion(f32[3,1024,256]{2,1,0:T(8,128)} %bitcast.163, f32[16,3,1024]{2,0,1:T(8,128)S(1)} %get-tuple-element.193), kind=kOutput, calls=%fused_computation.163 | convolution fusion | flops 150994944 | bytes 3391488 | tf_op jit(solution)/shard_map/awj,wjb->awb/dot_general | solution.py:10
  166.0 33.5 %all-gather = f32[256,3,256]{2,0,1:T(8,128)S(1)} all-gather(f32[16,3,256]{2,0,1:T(8,128)S(1)} %convolution_bitcast_fusion), channel_id=2, replica_groups=mesh['pole'=2,'prow'=16,'pcol'=16] {'prow'}, dimensions={0}, use_global_device_ids=true | all-gather | bytes 835584 | tf_op jit(solution)/shard_map/all_gather | solution.py:86
  (81 shorter events, 11.4 us)
Async XLA Ops:
  7.2 4.1 %copy-start = (f32[3,256,256]{2,1,0:T(8,128)S(1)}, f32[3,256,256]{2,1,0:T(8,128)}, u32[]{:S(2)}) copy-start(f32[3,256,256]{2,1,0:T(8,128)} %param.13) | copy-start | bytes 2359300
  7.2 45.5 %copy-start.5 = (s32[2]{0:T(128)S(1)}, s32[2]{0:T(128)}, u32[]{:S(2)}) copy-start(s32[2]{0:T(128)} %constant.361.clone) | copy-start | bytes 28
  7.2 155.1 %all-gather.3.cloned.1.call-start = ((), (), s32[]{:S(2)}) async-start(), calls=%async_computation.6 | async-start | bytes 3342336 | tf_op jit(solution)/shard_map/all_gather | solution.py:52
  59.9 32.1 %all-to-all-start.1 = ((f32[16,8,16,256]{3,2,1,0:T(8,128)}), f32[16,8,16,256]{3,2,1,0:T(8,128)S(1)}, u32[]{:S(2)}, u32[]{:S(2)}) async-start(f32[16,8,16,256]{3,2,1,0:T(8,128)} %broadcast_select_fusion.1), calls=%async_computation.1 | async-start | bytes 4194304 | tf_op jit(solution)/shard_map/cond/branch_1_fun/all_to_all | solution.py:63
  92.0 1.4 copy-start.2
  136.3 24.7 %all-to-all-start.4 = ((f32[16,16,8,256]{3,1,2,0:T(8,128)}), f32[16,16,8,256]{3,1,2,0:T(8,128)S(1)}, u32[]{:S(2)}, u32[]{:S(2)}) async-start(f32[16,16,8,256]{3,1,2,0:T(8,128)} %copy_select_fusion.1), calls=%async_computation.4 | async-start | bytes 4194304 | tf_op jit(solution)/shard_map/cond/branch_1_fun/all_to_all | solution.py:74
  162.2 38.0 %copy-start.3 = (f32[16,3,1024]{2,0,1:T(8,128)}, f32[16,3,1024]{2,0,1:T(8,128)S(1)}, u32[]{:S(2)}) copy-start(f32[16,3,1024]{2,0,1:T(8,128)S(1)} %get-tuple-element.193) | copy-start | bytes 589828
  162.2 37.3 %copy-start.4 = (f32[16,3,256]{2,0,1:T(8,128)S(1)}, f32[16,3,256]{2,0,1:T(8,128)}, u32[]{:S(2)}) copy-start(f32[16,3,256]{2,0,1:T(8,128)} %param.14) | copy-start | bytes 147460
  162.2 38.0 %copy-start.1 = (f32[3,256,256]{2,1,0:T(8,128)S(1)}, f32[3,256,256]{2,1,0:T(8,128)}, u32[]{:S(2)}) copy-start(f32[3,256,256]{2,1,0:T(8,128)} %param.13) | copy-start | bytes 2359300
Sparse Core Ops, SparseCore 0:
  50.6 70.2 all-gather.2
